TPU v7x, 256 devices: a whole 4x4x8 slice. The times are simulated.
256 devices in a mesh: grp: 4 (over y_lo, core), shard: 64 (over z, x, y_hi).
Axes of the slice: x: 4, y: 4 (y_hi: 2, y_lo: 2; y = y_hi * 2 + y_lo), z: 8, core: 2. Of those that a mesh axis runs over, the one named last changes fastest.
Arguments:
- layer_inner: float32 [4, 1600, 1600], P('grp', 'shard'), may hold values from -6 to 6
- layer_weights: float32 [1600, 1600], P('shard'), may hold values from -6 to 6
- layer_moment: float32 [1600, 1600], P('shard'), may hold values from -6 to 6
- embed_inner: float32 [4, 25600, 1600], P('grp', 'shard'), may hold values from -6 to 6
- embed_weights: float32 [25600, 1600], P(('shard', 'grp')), may hold values from -6 to 6
- embed_moment: float32 [25600, 1600], P(('shard', 'grp')), may hold values from -6 to 6
- basis: float32 [1600, 64], replicated, may hold values from -0.15625 to 0.15625
Outputs:
- layer_new: float32 [1600, 1600], P('shard')
- layer_moment_new: float32 [1600, 1600], P('shard')
- layer_copy: bfloat16 [1600, 1600], replicated
- embed_new: float32 [25600, 1600], P(('shard', 'grp'))
- embed_moment_new: float32 [25600, 1600], P(('shard', 'grp'))
All inputs are finite; a program needn't handle non-finite values.
Results may differ from a plain program's by a relative error of at most 0.0015.
Values may be sent and summed in bfloat16 or wider, within the bound.
No kernel may reach another device: no remote copies, remote signals or barrier semaphores. Data moves between devices by JAX's collectives and lax.ppermute only.
A program may use at most 128 MiB of HBM per device.

v0:
```python
import jax
import jax.numpy as jnp
from jax import lax
from jax.sharding import PartitionSpec as P

outer_rate = 0.7
momentum_coef = 0.9


def nesterov(weights, moment, average):
    moment_new = momentum_coef * moment + average
    return (weights - outer_rate * (average + momentum_coef * moment_new), moment_new)


def per_device(
    layer_inner, layer_weights, layer_moment, embed_inner, embed_weights, embed_moment, basis
):
    groups = lax.axis_size("grp")
    inner_proj = jnp.dot(embed_inner[0], basis, precision=lax.Precision.HIGHEST)
    mean_proj = (
        lax.psum_scatter(
            inner_proj.astype(jnp.bfloat16), "grp", scatter_dimension=0, tiled=True
        ).astype(jnp.float32)
        / groups
    )
    factors = jnp.dot(embed_weights, basis, precision=lax.Precision.HIGHEST) - mean_proj
    embed_step = jnp.dot(factors, basis.T, precision=lax.Precision.HIGHEST)
    embed_new, embed_moment_new = nesterov(embed_weights, embed_moment, embed_step)
    own_diff = layer_weights - layer_inner[0]
    average = lax.psum(own_diff, "grp") / groups
    layer_new, layer_moment_new = nesterov(layer_weights, layer_moment, average)
    layer_copy = lax.all_gather(layer_new.astype(jnp.bfloat16), "shard", axis=0, tiled=True)
    return (layer_new, layer_moment_new, layer_copy, embed_new, embed_moment_new)


def solution(mesh):
    in_specs = (
        P("grp", "shard", None),
        P("shard", None),
        P("shard", None),
        P("grp", "shard", None),
        P(("shard", "grp"), None),
        P(("shard", "grp"), None),
        P(),
    )
    out_specs = (
        P("shard", None),
        P("shard", None),
        P(),
        P(("shard", "grp"), None),
        P(("shard", "grp"), None),
    )
    return jax.shard_map(
        per_device, mesh=mesh, in_specs=in_specs, out_specs=out_specs, check_vma=False
    )
```

profile of v0, /device:TPU:2, one launch (start us, length us, event | category | flops | bytes accessed | tf_op | source)
XLA Modules:
  0.0 215.2 jit_solution(13905958962458578667)
XLA Ops:
  7.2 0.0 copy-start
  7.2 0.0 copy-start.1
  7.2 0.0 all-reduce.4.cloned.1.call-start
  7.2 1.9 bitcast_subtract_fusion
  9.1 0.0 all-reduce.4.cloned.1.call-update
  9.1 0.0 all-gather.3.cloned.1.call-start
  9.2 46.2 %all-reduce.4.cloned.1.call-done = f32[25,1600]{1,0:T(8,128)} async-done(((f32[25,1600]{1,0:T(8,128)}), f32[25,1600]{1,0:T(8,128)}) %all-reduce.4.cloned.1.call-update) | async-done | bytes 160016 | tf_op jit(solution)/shard_map/psum | solution.py:30
  55.4 2.0 convert_bitcast_fusion
  57.4 0.0 copy-start.2
  57.4 0.0 all-gather.3.cloned.1.call-update
  57.4 0.0 copy-done
  57.4 3.6 %fusion.3 = bf16[400,64]{0,1:T(8,128)(2,1)S(1)} fusion(f32[1600,64]{0,1:T(8,128)} %param.13, f32[1,400,1600]{2,1,0:T(8,128)S(1)} %copy-done), kind=kOutput, calls=%fused_computation.2 | convolution fusion | flops 491545600 | bytes 3020800 | tf_op jit(solution)/shard_map/dot_general | solution.py:19
  61.0 0.1 copy.12
  61.2 8.3 %fusion = bf16[112,64]{1,0:T(8,128)(2,1)S(1)} fusion(bf16[400,64]{1,0:T(8,128)(2,1)S(1)} %copy.12), kind=kCustom, calls=%all-reduce-scatter | all-reduce-scatter fusion | flops 28673 | bytes 66560
  69.5 1.3 collective-permute-start
  70.8 0.0 copy-done.1
  70.8 2.0 fusion.12
  72.7 0.0 copy-done.2
  72.7 0.6 dynamic-slice.4
  74.0 0.0 collective-permute-done
  74.0 0.3 concatenate
  74.3 0.1 copy.13
  74.4 3.3 %multiply_subtract_fusion = (f32[100,1600]{1,0:T(8,128)}, f32[100,1600]{1,0:T(8,128)}) fusion(f32[100,1600]{1,0:T(8,128)} %param.11, f32[100,1600]{1,0:T(8,128)} %param.12, f32[1600,64]{0,1:T(8,128)S(1)} %copy-done.1, f32[100,64]{0,1:T(8,128)S(1)} %fusion.12, bf16[100,64]{0,1:T(8,128)(2,1)S(1)} %copy.13), kind=kOutput, calls=%fused_computation.3 | convolution fusion | flops 123859200 | bytes 3008000 | tf_op jit(solution)/shard_map/dot_general | solution.py:27
  77.6 122.1 %all-gather.3.cloned.1.call-done = bf16[64,25,1600]{2,1,0:T(8,128)(2,1)} async-done(((bf16[1,25,1600]{2,1,0:T(8,128)(2,1)}), bf16[64,25,1600]{2,1,0:T(8,128)(2,1)}) %all-gather.3.cloned.1.call-update) | async-done | bytes 5120016 | tf_op jit(solution)/shard_map/all_gather | solution.py:32
  199.7 8.6 %reshape.11 = bf16[1600,1600]{1,0:T(8,128)(2,1)} reshape(bf16[64,25,1600]{2,1,0:T(8,128)(2,1)} %all-gather.3.cloned.1.call-done) | data formatting | bytes 10240000
  (2 shorter events, 0.0 us)
Async XLA Ops:
  7.2 50.2 %copy-start = (f32[1,400,1600]{2,1,0:T(8,128)S(1)}, f32[1,400,1600]{2,1,0:T(8,128)}, u32[]{:S(2)}) copy-start(f32[1,400,1600]{2,1,0:T(8,128)} %param.10) | copy-start | bytes 7680004
  7.2 63.6 %copy-start.1 = (f32[1600,64]{0,1:T(8,128)S(1)}, f32[1600,64]{0,1:T(8,128)}, u32[]{:S(2)}) copy-start(f32[1600,64]{0,1:T(8,128)} %param.13) | copy-start | bytes 1228804
  7.2 48.2 %all-reduce.4.cloned.1.call-start = ((), (), s32[]{:S(2)}) async-start(), calls=%async_computation | async-start | bytes 425984 | tf_op jit(solution)/shard_map/psum | solution.py:30
  9.1 190.6 %all-gather.3.cloned.1.call-start = ((), (), s32[]{:S(2)}) async-start(), calls=%async_computation.1 | async-start | bytes 6922240 | tf_op jit(solution)/shard_map/all_gather | solution.py:32
  57.4 15.4 %copy-start.2 = (u32[256]{0:T(256)S(1)}, u32[256]{0:T(256)}, u32[]{:S(2)}) copy-start(u32[256]{0:T(256)} %constant.19) | copy-start | bytes 3076
  69.5 4.5 %collective-permute-start = (bf16[36,64]{1,0:T(8,128)(2,1)S(1)}, bf16[36,64]{1,0:T(8,128)(2,1)S(1)}, u32[]{:S(2)}, u32[]{:S(2)}) collective-permute-start(bf16[36,64]{1,0:T(8,128)(2,1)S(1)} %slice), channel_id=1, source_target_pairs={{0,64},{64,128},{128,192},{1,65},{65,129},{129,193},{2,66},{66,130... | collective-permute-start | bytes 13832
Sparse Core Ops, SparseCore 0:
  11.2 44.1 all-reduce.3
  59.6 140.0 all-gather.2
where the time goes:
time: 216 us; the launch traced here: 215 us
  waiting for transfers between devices  168 us (78%)
  between operations  14.8 us (7%)
  local copies, waits for them, and re-layouts  9.74 us (5%)
  matrix products  8.84 us (4%)
  blocking collectives  8.27 us (4%)
  other arithmetic  3.85 us (2%)
    all_gather x1, waiting for transfers between devices, per_device(): lax.all_gather(layer_new.astype(jnp.bfloat16), 'shard', axis=0, tiled=True)  122 us
    psum x1, waiting for transfers between devices, per_device(): average = lax.psum(own_diff, 'grp') / groups  46.2 us
    unnamed x11, local copies, waits for them, and re-layouts  9.52 us
    unnamed x1, blocking collectives  8.27 us
  transfers between devices with their start and end apart: 3, of which 2 were waited for; matrix products, arithmetic and copies ran while one was open for 8% of the time, Pallas kernels for 0%

commit v1 on v0

--- a/solution.py
+++ b/solution.py
@@ -1,10 +1,20 @@
+import functools
 import jax
 import jax.numpy as jnp
 from jax import lax
 from jax.sharding import PartitionSpec as P
+from jax.lax import all_gather
 
 outer_rate = 0.7
 momentum_coef = 0.9
+
+
+def fill_object(sheet, device_axis):
+    long_array = jnp.sum(all_gather(sheet, device_axis), axis=0)
+    return long_array
+
+
+_order_figure = functools.partial(fill_object, device_axis="grp")
 
 
 def nesterov(weights, moment, average):
@@ -27,7 +37,7 @@
     embed_step = jnp.dot(factors, basis.T, precision=lax.Precision.HIGHEST)
     embed_new, embed_moment_new = nesterov(embed_weights, embed_moment, embed_step)
     own_diff = layer_weights - layer_inner[0]
-    average = lax.psum(own_diff, "grp") / groups
+    average = _order_figure(own_diff) / groups
     layer_new, layer_moment_new = nesterov(layer_weights, layer_moment, average)
     layer_copy = lax.all_gather(layer_new.astype(jnp.bfloat16), "shard", axis=0, tiled=True)
     return (layer_new, layer_moment_new, layer_copy, embed_new, embed_moment_new)

time: 216 us -> 179 us (0.83)
  waiting for transfers between devices: 168 us -> 123 us
  blocking collectives: 8.27 us -> 17.8 us
    psum x1 -> x0, waiting for transfers between devices: 46.2 us -> none  [per_device(): average = lax.psum(own_diff, 'grp') / groups]
    all_gather x0 -> x1, blocking collectives: none -> 9.49 us  [fill_object(): long_array = jnp.sum(all_gather(sheet, device_axis), axis=0)]
    unnamed x11 -> x13, local copies, waits for them, and re-layouts: 9.52 us -> 9.52 us
  transfers between devices with their start and end apart: 3 -> 2, of which waited for: 2 -> 1; matrix products, arithmetic and copies ran while one was open for 8% -> 10% of each run, Pallas kernels for 0% -> 0%
where the time goes in v1:
time: 179 us; the launch traced here: 178 us
  waiting for transfers between devices  123 us (69%)
  blocking collectives  17.8 us (10%)
  between operations  14.8 us (8%)
  local copies, waits for them, and re-layouts  9.74 us (5%)
  matrix products  7.87 us (4%)
  other arithmetic  4.25 us (2%)
    all_gather x1, waiting for transfers between devices, per_device(): lax.all_gather(layer_new.astype(jnp.bfloat16), 'shard', axis=0, tiled=True)  123 us
    unnamed x13, local copies, waits for them, and re-layouts  9.52 us
    all_gather x1, blocking collectives, fill_object(): long_array = jnp.sum(all_gather(sheet, device_axis), axis=0)  9.49 us
    unnamed x1, blocking collectives  8.27 us
  transfers between devices with their start and end apart: 2, of which 1 were waited for; matrix products, arithmetic and copies ran while one was open for 10% of the time, Pallas kernels for 0%

profile of v1, /device:TPU:2, one launch (start us, length us, event | category | flops | bytes accessed | tf_op | source)
XLA Modules:
  0.0 178.3 jit_solution(7045176719534472360)
XLA Ops:
  7.2 0.0 copy-start
  7.2 0.0 copy-start.2
  7.2 0.0 copy-start.1
  7.2 0.0 all-gather.5.cloned.1.call-start
  7.2 1.2 fusion.6
  8.5 9.5 %all-gather.1 = f32[4,25,1600]{2,1,0:T(8,128)} all-gather(f32[1,25,1600]{2,1,0:T(8,128)S(1)} %fusion.6), channel_id=2, replica_groups=mesh['grp'=4,'shard'=64] {'grp'}, dimensions={0}, use_global_device_ids=true | all-gather | bytes 800000 | tf_op jit(solution)/shard_map/all_gather | solution.py:13
  18.0 1.2 reduce_sum.9
  19.2 0.0 copy-done.2
  19.2 1.8 %convert_bitcast_fusion = (bf16[1,25,1600]{2,1,0:T(8,128)(2,1)}, f32[25,1600]{1,0:T(8,128)}, f32[25,1600]{1,0:T(8,128)}) fusion(f32[25,1600]{1,0:T(8,128)S(1)} %copy-done.2, f32[25,1600]{1,0:T(8,128)S(1)} %reduce_sum.9, f32[25,1600]{1,0:T(8,128)} %param.9), kind=kLoop, calls=%fused_computation.9 | loop fusion | flops 320000 | bytes 880000
  21.0 0.0 copy-start.3
  21.0 0.0 all-gather.5.cloned.1.call-update
  21.0 0.0 copy-done
  21.0 0.0 copy-done.1
  21.0 2.6 %fusion.3 = bf16[400,64]{0,1:T(8,128)(2,1)S(1)} fusion(f32[1600,64]{0,1:T(8,128)S(1)} %copy-done.1, f32[1,400,1600]{2,1,0:T(8,128)S(1)} %copy-done), kind=kOutput, calls=%fused_computation.2 | convolution fusion | flops 491545600 | bytes 3020800 | tf_op jit(solution)/shard_map/dot_general | solution.py:29
  23.7 0.1 copy.12
  23.8 8.3 %fusion = bf16[112,64]{1,0:T(8,128)(2,1)S(1)} fusion(bf16[400,64]{1,0:T(8,128)(2,1)S(1)} %copy.12), kind=kCustom, calls=%all-reduce-scatter | all-reduce-scatter fusion | flops 28673 | bytes 66560
  32.1 1.3 collective-permute-start
  33.4 2.0 %fusion.13 = f32[100,64]{0,1:T(8,128)S(1)} fusion(f32[100,1600]{1,0:T(8,128)} %param.11, f32[1600,64]{0,1:T(8,128)S(1)} %copy-done.1), kind=kOutput, calls=%fused_computation.17 | convolution fusion | flops 122880000 | bytes 1075200 | tf_op jit(solution)/shard_map/dot_general | solution.py:36
  35.4 0.0 copy-done.3
  35.4 0.6 dynamic-slice.4
  36.6 0.0 collective-permute-done
  36.6 0.3 concatenate
  36.9 0.1 copy.13
  37.0 3.3 %multiply_subtract_fusion = (f32[100,1600]{1,0:T(8,128)}, f32[100,1600]{1,0:T(8,128)}) fusion(f32[100,1600]{1,0:T(8,128)} %param.11, f32[100,1600]{1,0:T(8,128)} %param.12, f32[1600,64]{0,1:T(8,128)S(1)} %copy-done.1, f32[100,64]{0,1:T(8,128)S(1)} %fusion.13, bf16[100,64]{0,1:T(8,128)(2,1)S(1)} %copy.13), kind=kOutput, calls=%fused_computation.3 | convolution fusion | flops 123859200 | bytes 3008000 | tf_op jit(solution)/shard_map/dot_general | solution.py:37
  40.3 122.5 %all-gather.5.cloned.1.call-done = bf16[64,25,1600]{2,1,0:T(8,128)(2,1)} async-done(((bf16[1,25,1600]{2,1,0:T(8,128)(2,1)}), bf16[64,25,1600]{2,1,0:T(8,128)(2,1)}) %all-gather.5.cloned.1.call-update) | async-done | bytes 5120016 | tf_op jit(solution)/shard_map/all_gather | solution.py:42
  162.8 8.6 %reshape.14 = bf16[1600,1600]{1,0:T(8,128)(2,1)} reshape(bf16[64,25,1600]{2,1,0:T(8,128)(2,1)} %all-gather.5.cloned.1.call-done) | data formatting | bytes 10240000
  (2 shorter events, 0.0 us)
Async XLA Ops:
  7.2 13.9 %copy-start = (f32[1,400,1600]{2,1,0:T(8,128)S(1)}, f32[1,400,1600]{2,1,0:T(8,128)}, u32[]{:S(2)}) copy-start(f32[1,400,1600]{2,1,0:T(8,128)} %param.10) | copy-start | bytes 7680004
  7.2 12.0 %copy-start.2 = (f32[25,1600]{1,0:T(8,128)S(1)}, f32[25,1600]{1,0:T(8,128)}, u32[]{:S(2)}) copy-start(f32[25,1600]{1,0:T(8,128)} %param.8) | copy-start | bytes 480004
  7.2 13.8 %copy-start.1 = (f32[1600,64]{0,1:T(8,128)S(1)}, f32[1600,64]{0,1:T(8,128)}, u32[]{:S(2)}) copy-start(f32[1600,64]{0,1:T(8,128)} %param.13) | copy-start | bytes 1228804
  7.2 155.6 %all-gather.5.cloned.1.call-start = ((), (), s32[]{:S(2)}) async-start(), calls=%async_computation | async-start | bytes 6922240 | tf_op jit(solution)/shard_map/all_gather | solution.py:42
  21.0 14.4 %copy-start.3 = (u32[256]{0:T(256)S(1)}, u32[256]{0:T(256)}, u32[]{:S(2)}) copy-start(u32[256]{0:T(256)} %constant.21) | copy-start | bytes 3076
  32.1 4.5 %collective-permute-start = (bf16[36,64]{1,0:T(8,128)(2,1)S(1)}, bf16[36,64]{1,0:T(8,128)(2,1)S(1)}, u32[]{:S(2)}, u32[]{:S(2)}) collective-permute-start(bf16[36,64]{1,0:T(8,128)(2,1)S(1)} %slice), channel_id=1, source_target_pairs={{0,64},{64,128},{128,192},{1,65},{65,129},{129,193},{2,66},{66,130... | collective-permute-start | bytes 13832
Sparse Core Ops, SparseCore 0:
  21.1 141.6 all-gather.4

commit v2 on v0

--- a/solution.py
+++ b/solution.py
@@ -29,7 +29,9 @@
     own_diff = layer_weights - layer_inner[0]
     average = lax.psum(own_diff, "grp") / groups
     layer_new, layer_moment_new = nesterov(layer_weights, layer_moment, average)
-    layer_copy = lax.all_gather(layer_new.astype(jnp.bfloat16), "shard", axis=0, tiled=True)
+    x = layer_new.astype(jnp.bfloat16)
+    sent = jnp.stack([x] * lax.axis_size("shard"))
+    layer_copy = jnp.concatenate(lax.all_to_all(sent, "shard", 0, 0), axis=0)
     return (layer_new, layer_moment_new, layer_copy, embed_new, embed_moment_new)
 
 

time: 216 us -> 248 us (1.15)
  the two profiles are of different devices: /device:TPU:2 before, /device:TPU:9 now
where the time goes in v2:
time: 248 us; the launch traced here: 247 us
  waiting for transfers between devices  177 us (71%)
  blocking collectives  18 us (7%)
  between operations  14.8 us (6%)
  starting transfers between devices  13.3 us (5%)
  local copies, waits for them, and re-layouts  13.1 us (5%)
  matrix products  7.84 us (3%)
  other arithmetic  3.82 us (2%)
    all_to_all x1, waiting for transfers between devices, per_device(): layer_copy = jnp.concatenate(lax.all_to_all(sent, 'shard', 0, 0), axis=0)  130 us
    psum x1, waiting for transfers between devices, per_device(): average = lax.psum(own_diff, 'grp') / groups  46.1 us
    unnamed x1, blocking collectives  18 us
    all_to_all x1, starting transfers between devices, per_device(): layer_copy = jnp.concatenate(lax.all_to_all(sent, 'shard', 0, 0), axis=0)  12 us
    reshape x1, local copies, waits for them, and re-layouts, per_device(): layer_copy = jnp.concatenate(lax.all_to_all(sent, 'shard', 0, 0), axis=0)  8.62 us
  transfers between devices with their start and end apart: 3, of which 2 were waited for; matrix products, arithmetic and copies ran while one was open for 11% of the time, Pallas kernels for 0%

profile of v2, /device:TPU:9, one launch (start us, length us, event | category | flops | bytes accessed | tf_op | source)
XLA Modules:
  0.0 247.4 jit_solution(5900573409434700661)
XLA Ops:
  7.2 0.0 copy-start
  7.2 0.0 all-reduce.4.cloned.1.call-start
  7.2 1.9 bitcast_subtract_fusion
  9.1 0.0 all-reduce.4.cloned.1.call-update
  9.1 46.1 %all-reduce.4.cloned.1.call-done = f32[25,1600]{1,0:T(8,128)} async-done(((f32[25,1600]{1,0:T(8,128)}), f32[25,1600]{1,0:T(8,128)}) %all-reduce.4.cloned.1.call-update) | async-done | bytes 160016 | tf_op jit(solution)/shard_map/psum | solution.py:30
  55.3 1.9 fusion.12
  57.2 3.3 %stack.2 = bf16[64,25,1600]{2,1,0:T(8,128)(2,1)} broadcast(bf16[25,1600]{1,0:T(8,128)(2,1)S(1)} %get-tuple-element.7), dimensions={1,2} | broadcast | bytes 5200000 | tf_op jit(solution)/shard_map/stack | solution.py:33
  60.5 0.0 copy-start.1
  60.5 12.0 %all-to-all-start = ((bf16[64,25,1600]{2,1,0:T(8,128)(2,1)}), bf16[64,25,1600]{2,1,0:T(8,128)(2,1)}, u32[]{:S(2)}, u32[]{:S(2)}) async-start(bf16[64,25,1600]{2,1,0:T(8,128)(2,1)} %stack.2), calls=%async_computation | async-start | bytes 13631488 | tf_op jit(solution)/shard_map/all_to_all | solution.py:34
  72.6 0.0 copy-done
  72.6 0.0 copy-done.1
  72.6 0.0 copy-start.2
  72.6 2.6 %fusion.3 = bf16[400,64]{0,1:T(8,128)(2,1)S(1)} fusion(f32[1600,64]{0,1:T(8,128)S(1)} %copy-done.1, f32[1,400,1600]{2,1,0:T(8,128)S(1)} %copy-done), kind=kOutput, calls=%fused_computation.2 | convolution fusion | flops 491545600 | bytes 3020800 | tf_op jit(solution)/shard_map/dot_general | solution.py:19
  75.2 0.1 copy.12
  75.3 18.0 %fusion = bf16[112,64]{1,0:T(8,128)(2,1)S(1)} fusion(bf16[400,64]{1,0:T(8,128)(2,1)S(1)} %copy.12), kind=kCustom, calls=%all-reduce-scatter | all-reduce-scatter fusion | flops 28673 | bytes 66560
  93.4 1.3 collective-permute-start
  94.7 2.0 fusion.13
  96.7 0.0 copy-done.2
  96.7 0.6 dynamic-slice.4
  97.9 0.0 collective-permute-done
  97.9 0.3 concatenate
  98.2 0.1 copy.13
  98.3 3.2 %multiply_subtract_fusion = (f32[100,1600]{1,0:T(8,128)}, f32[100,1600]{1,0:T(8,128)}) fusion(f32[100,1600]{1,0:T(8,128)} %param.11, f32[100,1600]{1,0:T(8,128)} %param.12, f32[1600,64]{0,1:T(8,128)S(1)} %copy-done.1, f32[100,64]{0,1:T(8,128)S(1)} %fusion.13, bf16[100,64]{0,1:T(8,128)(2,1)S(1)} %copy.13), kind=kOutput, calls=%fused_computation.3 | convolution fusion | flops 123859200 | bytes 3008000 | tf_op jit(solution)/shard_map/dot_general | solution.py:27
  101.6 130.4 %all-to-all-done = bf16[64,25,1600]{2,1,0:T(8,128)(2,1)} async-done(((bf16[64,25,1600]{2,1,0:T(8,128)(2,1)}), bf16[64,25,1600]{2,1,0:T(8,128)(2,1)}, u32[]{:S(2)}, u32[]{:S(2)}) %all-to-all-start) | async-done | bytes 5120032 | tf_op jit(solution)/shard_map/all_to_all | solution.py:34
  232.0 8.6 %reshape.15 = bf16[1600,1600]{1,0:T(8,128)(2,1)} reshape(bf16[64,25,1600]{2,1,0:T(8,128)(2,1)} %all-to-all-done) | data formatting | bytes 10240000 | tf_op jit(solution)/shard_map/reshape | solution.py:34
  (2 shorter events, 0.0 us)
Async XLA Ops:
  7.2 65.4 %copy-start = (f32[1,400,1600]{2,1,0:T(8,128)S(1)}, f32[1,400,1600]{2,1,0:T(8,128)}, u32[]{:S(2)}) copy-start(f32[1,400,1600]{2,1,0:T(8,128)} %param.10) | copy-start | bytes 7680004
  7.2 48.1 %all-reduce.4.cloned.1.call-start = ((), (), s32[]{:S(2)}) async-start(), calls=%async_computation.1 | async-start | bytes 425984 | tf_op jit(solution)/shard_map/psum | solution.py:30
  60.5 12.0 %copy-start.1 = (f32[1600,64]{0,1:T(8,128)S(1)}, f32[1600,64]{0,1:T(8,128)}, u32[]{:S(2)}) copy-start(f32[1600,64]{0,1:T(8,128)} %param.13) | copy-start | bytes 1228804
  60.5 171.4 %all-to-all-start = ((bf16[64,25,1600]{2,1,0:T(8,128)(2,1)}), bf16[64,25,1600]{2,1,0:T(8,128)(2,1)}, u32[]{:S(2)}, u32[]{:S(2)}) async-start(bf16[64,25,1600]{2,1,0:T(8,128)(2,1)} %stack.2), calls=%async_computation | async-start | bytes 13631488 | tf_op jit(solution)/shard_map/all_to_all | solution.py:34
  72.6 24.1 %copy-start.2 = (u32[256]{0:T(256)S(1)}, u32[256]{0:T(256)}, u32[]{:S(2)}) copy-start(u32[256]{0:T(256)} %constant.19) | copy-start | bytes 3076
  93.4 4.5 %collective-permute-start = (bf16[36,64]{1,0:T(8,128)(2,1)S(1)}, bf16[36,64]{1,0:T(8,128)(2,1)S(1)}, u32[]{:S(2)}, u32[]{:S(2)}) collective-permute-start(bf16[36,64]{1,0:T(8,128)(2,1)S(1)} %slice), channel_id=1, source_target_pairs={{0,64},{64,128},{128,192},{1,65},{65,129},{129,193},{2,66},{66,130... | collective-permute-start | bytes 13832
Sparse Core Ops, SparseCore 0:
  11.2 44.0 all-reduce.3
